TPU v7x, 32 devices: a whole 2x2x4 slice. The times are simulated.
32 devices in a mesh: freq: 4 (over z), blk: 8 (over y, x, core).
Axes of the slice: x: 2, y: 2, z: 4, core: 2. Of those that a mesh axis runs over, the one named last changes fastest.
Arguments:
- spectra: bfloat16 [8, 512, 2, 32, 128], P('blk', 'freq'), may hold values from -6 to 6
- pair_offsets: int32 [8, 5], P('blk'), may hold values from 0 to 4, as said below
- pair_count: int32 [8], P('blk'), may hold values from 1 to 5, as said below
Outputs:
- correlations: bfloat16 [8, 5, 128, 256, 128], P('blk', None, 'freq')
Inputs may be any that keep to these rules, and one draw needn't show every extreme that they name: `pair_offsets`: for every block, slot 0 holds 0 (the block with itself) and slots 1 to 4 hold the offsets 1 to 4, each once, in an order drawn for each block. `pair_count`: slots at or beyond a block's count are unused; block 0 lists every slot.
All inputs are finite; a program needn't handle non-finite values.
Results may differ from a plain program's by a relative error of at most 0.0052.
Values may be sent and summed in bfloat16 or wider, within the bound.
No kernel may reach another device: no remote copies, remote signals or barrier semaphores. Data moves between devices by JAX's collectives and lax.ppermute only.
A program may use at most 192 MiB of HBM per device.

v0:
```python
import math
import jax
import jax.numpy as jnp
from jax import lax
from jax.sharding import PartitionSpec as P

F = 512
LAGS = 256
REACH = 4
SLOTS = 5


def from_behind(shard, axis, by):
    size = lax.axis_size(axis)
    return lax.ppermute(shard, axis, [(i, (i + by) % size) for i in range(size)])


def lag_table():
    shifted = jnp.arange(LAGS, dtype=jnp.int32) - LAGS // 2
    bins = jnp.arange(F, dtype=jnp.int32) + 1
    phase = jnp.mod(shifted[:, None] * bins[None, :], 2 * F).astype(jnp.float32) * (jnp.pi / F)
    return jnp.stack([jnp.cos(phase), -jnp.sin(phase)], axis=-1).astype(jnp.bfloat16)


def cross_spectrum(home_spec, partner):
    freq_count, parts_count, windows, stations = home_spec.shape
    row_matrix = home_spec.reshape(freq_count, 2 * windows, stations)
    real_part = partner[:, 0]
    imag_part = partner[:, 1]
    real_rows = jnp.concatenate([real_part, imag_part], axis=1)
    imag_rows = jnp.concatenate([imag_part, -real_part], axis=1)
    column_matrix = jnp.concatenate([real_rows, imag_rows], axis=2)
    summed = jnp.einsum(
        "fks,fkt->fst", row_matrix, column_matrix, preferred_element_type=jnp.float32
    )
    return summed / windows


def local(spectra, pair_offsets, pair_count):
    home_spec = spectra[0]
    fetched = [home_spec]
    for offset_step in range(1, REACH + 1):
        fetched.append(from_behind(home_spec, "blk", -offset_step))
    nearby = jnp.stack(fetched)
    partner_offsets = pair_offsets[0]
    listed = pair_count[0]

    def slot_cross(slot_index):
        partner = lax.dynamic_index_in_dim(nearby, partner_offsets[slot_index], 0, keepdims=False)
        cross_term = cross_spectrum(home_spec, partner)
        return jnp.where(slot_index < listed, cross_term, 0.0).astype(jnp.bfloat16)

    crosses = jnp.stack([slot_cross(slot_index) for slot_index in range(SLOTS)])
    lag_weights = lag_table()
    grouped = lax.all_to_all(crosses, "freq", split_axis=2, concat_axis=1, tiled=True)
    count_slots, freq_total, stations_part, double_width = grouped.shape
    regrouped = grouped.reshape(count_slots, freq_total, stations_part, 2, double_width // 2)
    lagged = jnp.einsum(
        "lfr,nfsrt->nslt", lag_weights, regrouped, preferred_element_type=jnp.float32
    )
    result = (lagged * math.sqrt(2.0 / freq_total)).astype(jnp.bfloat16)
    return result[None]


def solution(mesh):
    placed = (P("blk", "freq", None, None, None), P("blk", None), P("blk"))
    return jax.shard_map(
        local,
        mesh=mesh,
        in_specs=placed,
        out_specs=P("blk", None, "freq", None, None),
        check_vma=False,
    )
```

profile of v0, /device:TPU:6, one launch (start us, length us, event | category | flops | bytes accessed | tf_op | source)
XLA Modules:
  0.0 1326.5 jit_solution(1731177960773644525)
XLA Ops:
  14.5 3.3 constant_dynamic-update-slice_fusion
  17.9 28.4 %collective-permute-done = bf16[128,2,32,128]{3,2,1,0:T(8,128)(2,1)} collective-permute-done((bf16[128,2,32,128]{3,2,1,0:T(8,128)(2,1)}, bf16[128,2,32,128]{3,2,1,0:T(8,128)(2,1)}, u32[]{:S(2)}, u32[]{:S(2)}) %collective-permute-start) | collective-permute-done | bytes 2097184 | tf_op jit(solution)/shard_map/ppermute | solution.py:15
  46.3 3.3 bitcast_dynamic-update-slice_fusion.8
  49.6 44.5 %collective-permute-done.1 = bf16[128,2,32,128]{3,2,1,0:T(8,128)(2,1)} collective-permute-done((bf16[128,2,32,128]{3,2,1,0:T(8,128)(2,1)}, bf16[128,2,32,128]{3,2,1,0:T(8,128)(2,1)}, u32[]{:S(2)}, u32[]{:S(2)}) %collective-permute-start.1) | collective-permute-done | bytes 2097184 | tf_op jit(solution)/shard_map/ppermute | solution.py:15
  94.1 3.3 bitcast_dynamic-update-slice_fusion.7
  97.4 39.5 %collective-permute-done.2 = bf16[128,2,32,128]{3,2,1,0:T(8,128)(2,1)} collective-permute-done((bf16[128,2,32,128]{3,2,1,0:T(8,128)(2,1)}, bf16[128,2,32,128]{3,2,1,0:T(8,128)(2,1)}, u32[]{:S(2)}, u32[]{:S(2)}) %collective-permute-start.2) | collective-permute-done | bytes 2097184 | tf_op jit(solution)/shard_map/ppermute | solution.py:15
  137.0 3.3 bitcast_dynamic-update-slice_fusion.6
  140.3 21.1 %collective-permute-done.3 = bf16[128,2,32,128]{3,2,1,0:T(8,128)(2,1)S(1)} collective-permute-done((bf16[128,2,32,128]{3,2,1,0:T(8,128)(2,1)}, bf16[128,2,32,128]{3,2,1,0:T(8,128)(2,1)S(1)}, u32[]{:S(2)}, u32[]{:S(2)}) %collective-permute-start.3) | collective-permute-done | bytes 2097184 | tf_op jit(solution)/shard_map/ppermute | solution.py:15
  161.4 1.7 bitcast_dynamic-update-slice_fusion.5
  163.2 8.0 constant_dynamic-slice_fusion
  171.1 2.4 copy_bitcast_fusion.2
  183.9 7.0 bitcast_dynamic-update-slice_fusion.4
  191.0 6.8 bitcast_dynamic-update-slice_fusion.3
  197.8 6.9 bitcast_dynamic-update-slice_fusion.2
  204.7 6.9 bitcast_dynamic-update-slice_fusion.1
  211.6 5.4 bitcast_dynamic-update-slice_fusion
  217.0 55.5 %copy.24 = bf16[5,128,128,256]{3,1,0,2:T(8,128)(2,1)} copy(bf16[5,128,128,256]{2,3,1,0:T(8,128)(2,1)} %bitcast_dynamic-update-slice_fusion) | data formatting | bytes 83886080 | tf_op jit(solution)/shard_map/stack | solution.py:53
  272.5 11.4 all-to-all-start
  283.9 2.5 cosine_convert_fusion
  286.4 880.8 %all-to-all-done = bf16[5,128,128,256]{3,1,0,2:T(8,128)(2,1)} async-done(((bf16[5,128,128,256]{3,1,0,2:T(8,128)(2,1)}), bf16[5,128,128,256]{3,1,0,2:T(8,128)(2,1)}, u32[]{:S(2)}, u32[]{:S(2)}) %all-to-all-start) | async-done | bytes 41943072 | tf_op jit(solution)/shard_map/all_to_all | solution.py:55
  1167.2 62.7 %copy.26 = bf16[5,4,128,32,256]{2,1,4,3,0:T(4,128)(2,1)} copy(bf16[5,4,128,32,256]{4,2,0,3,1:T(8,128)(2,1)} %bitcast.43) | data formatting | bytes 83886080 | tf_op jit(solution)/shard_map/all_to_all | solution.py:55
  1229.9 60.3 %reshape.163 = bf16[5,512,32,2,128]{1,4,3,2,0:T(8,128)(2,1)} reshape(bf16[5,4,128,32,256]{2,1,4,3,0:T(4,128)(2,1)} %copy.26) | data formatting | bytes 83886080 | tf_op jit(solution)/shard_map/reshape | solution.py:57
  1290.2 22.1 %fusion.1 = bf16[1,5,32,256,128]{3,4,2,1,0:T(8,128)(2,1)} fusion(bf16[5,512,32,2,128]{1,4,3,2,0:T(8,128)(2,1)} %reshape.163, bf16[256,512,1]{1,0,2:T(8,128)(2,1)S(1)} %get-tuple-element.21, bf16[256,512,1]{1,0,2:T(8,128)(2,1)S(1)} %get-tuple-element.20), kind=kOutput, calls=%fused_computation.7 | convolution fusion | flops 10748166144 | bytes 52953088 | tf_op jit(solution)/shard_map/lfr,nfsrt->nslt/dot_general | solution.py:58
  1312.4 14.2 %copy.27 = bf16[1,5,32,256,128]{4,3,2,1,0:T(8,128)(2,1)} copy(bf16[1,5,32,256,128]{3,4,2,1,0:T(8,128)(2,1)} %fusion.1) | data formatting | bytes 20971520 | tf_op jit(solution)/shard_map/broadcast_in_dim | solution.py:62
  (27 shorter events, 14.8 us)
Async XLA Ops:
  0.0 46.3 %collective-permute-start = (bf16[128,2,32,128]{3,2,1,0:T(8,128)(2,1)}, bf16[128,2,32,128]{3,2,1,0:T(8,128)(2,1)}, u32[]{:S(2)}, u32[]{:S(2)}) collective-permute-start(bf16[128,2,32,128]{3,2,1,0:T(8,128)(2,1)} %bitcast.110), channel_id=1, source_target_pairs={{0,7},{1,0},{2,1},{3,2},{4,3},{5,4},{6,5},{7,6},{8,15},{9,8},{10,9... | collective-permute-start | bytes 6291464 | tf_op jit(solution)/shard_map/ppermute | solution.py:15
  0.0 94.1 %collective-permute-start.1 = (bf16[128,2,32,128]{3,2,1,0:T(8,128)(2,1)}, bf16[128,2,32,128]{3,2,1,0:T(8,128)(2,1)}, u32[]{:S(2)}, u32[]{:S(2)}) collective-permute-start(bf16[128,2,32,128]{3,2,1,0:T(8,128)(2,1)} %bitcast.111), channel_id=1, source_target_pairs={{0,6},{1,7},{2,0},{3,1},{4,2},{5,3},{6,4},{7,5},{8,14},{9,15},{10,... | collective-permute-start | bytes 6291464 | tf_op jit(solution)/shard_map/ppermute | solution.py:15
  1.4 135.6 %collective-permute-start.2 = (bf16[128,2,32,128]{3,2,1,0:T(8,128)(2,1)}, bf16[128,2,32,128]{3,2,1,0:T(8,128)(2,1)}, u32[]{:S(2)}, u32[]{:S(2)}) collective-permute-start(bf16[128,2,32,128]{3,2,1,0:T(8,128)(2,1)} %bitcast.112), channel_id=1, source_target_pairs={{0,5},{1,6},{2,7},{3,0},{4,1},{5,2},{6,3},{7,4},{8,13},{9,14},{10,... | collective-permute-start | bytes 6291464 | tf_op jit(solution)/shard_map/ppermute | solution.py:15
  1.4 160.0 %collective-permute-start.3 = (bf16[128,2,32,128]{3,2,1,0:T(8,128)(2,1)}, bf16[128,2,32,128]{3,2,1,0:T(8,128)(2,1)S(1)}, u32[]{:S(2)}, u32[]{:S(2)}) collective-permute-start(bf16[128,2,32,128]{3,2,1,0:T(8,128)(2,1)} %bitcast.113), channel_id=1, source_target_pairs={{0,4},{1,5},{2,6},{3,7},{4,0},{5,1},{6,2},{7,3},{8,12},{9,13},{10,... | collective-permute-start | bytes 6291464 | tf_op jit(solution)/shard_map/ppermute | solution.py:15
  180.2 3.7 copy-start
  190.9 6.8 copy-start.1
  204.7 6.9 copy-start.2
  204.7 6.9 copy-start.3
  272.5 894.7 %all-to-all-start = ((bf16[5,128,128,256]{3,1,0,2:T(8,128)(2,1)}), bf16[5,128,128,256]{3,1,0,2:T(8,128)(2,1)}, u32[]{:S(2)}, u32[]{:S(2)}) async-start(bf16[5,128,128,256]{3,1,0,2:T(8,128)(2,1)} %copy.24), calls=%async_computation | async-start | bytes 83886080 | tf_op jit(solution)/shard_map/all_to_all | solution.py:55
where the time goes:
time: 1330 us
  waiting for transfers between devices  1010 us (76%)
  local copies, waits for them, and re-layouts  229 us (17%)
  matrix products  55.2 us (4%)
  starting transfers between devices  14.4 us (1%)
    all_to_all x1, waiting for transfers between devices, local(): lax.all_to_all(crosses, 'freq', split_axis=2, concat_axis=1, tiled=True)  881 us
    ppermute x4, waiting for transfers between devices, from_behind(): lax.ppermute(shard, axis, [(i, (i + by) % size) for i in range(size)])  134 us
    all_to_all x1, local copies, waits for them, and re-layouts, local(): lax.all_to_all(crosses, 'freq', split_axis=2, concat_axis=1, tiled=True)  62.7 us
    reshape x1, local copies, waits for them, and re-layouts, local(): grouped.reshape(count_slots, freq_total, stations_part, 2, double_width /...  60.3 us
    another operation x1, local copies, waits for them, and re-layouts, local(): crosses = jnp.stack([slot_cross(slot_index) for slot_index in range(SLOTS)])  55.5 us
    dot_general x5, matrix products, cross_spectrum(): jnp.einsum('fks,fkt->fst', row_matrix, column_matrix, preferred_element_t...  33 us
  transfers between devices with their start and end apart: 5, of which 5 were waited for; matrix products, arithmetic and copies ran while one was open for 1% of the time, Pallas kernels for 0%

commit v1 on v0

--- a/solution.py
+++ b/solution.py
@@ -8,6 +8,20 @@
 LAGS = 256
 REACH = 4
 SLOTS = 5
+
+
+def guide_the_keys(arr_in, dim_at, obj):
+    left_arr = arr_in.shape
+    next_value = arr_in.reshape(
+        *left_arr[:dim_at], obj, left_arr[dim_at] // obj, *left_arr[dim_at + 1 :]
+    )
+    return jnp.moveaxis(next_value, dim_at, 0)
+
+
+def recast_the_chunk(m, row_dim):
+    m = jnp.moveaxis(m, 0, row_dim)
+    reply = m.shape
+    return m.reshape(*reply[:row_dim], reply[row_dim] * reply[row_dim + 1], *reply[row_dim + 2 :])
 
 
 def from_behind(shard, axis, by):
@@ -52,7 +66,18 @@
 
     crosses = jnp.stack([slot_cross(slot_index) for slot_index in range(SLOTS)])
     lag_weights = lag_table()
-    grouped = lax.all_to_all(crosses, "freq", split_axis=2, concat_axis=1, tiled=True)
+    piece_out = lax.axis_size("freq")
+    item_now = lax.axis_index("freq")
+    after, new = (piece_out, item_now)
+    extra = guide_the_keys(crosses, 2, after)
+    all_rows = [extra[new]]
+    for j0 in range(1, after):
+        r1 = extra[new ^ j0]
+        tmp = lax.ppermute(r1, axis_name="freq", perm=[(pp, pp ^ j0) for pp in range(after)])
+        all_rows.append(tmp)
+    low = jnp.stack(all_rows)
+    extra = low[new ^ jnp.arange(after)]
+    grouped = recast_the_chunk(extra, 1)
     count_slots, freq_total, stations_part, double_width = grouped.shape
     regrouped = grouped.reshape(count_slots, freq_total, stations_part, 2, double_width // 2)
     lagged = jnp.einsum(

time: 1330 us -> 1480 us (1.11)
  local copies, waits for them, and re-layouts: 229 us -> 333 us
  other arithmetic: 3.15 us -> 64.2 us
    all_to_all x1 -> x0, waiting for transfers between devices: 881 us -> none  [local(): lax.all_to_all(crosses, 'freq', split_axis=2, concat_axis=1, tiled=True)]
    ppermute x0 -> x3, waiting for transfers between devices: none -> 876 us  [local(): lax.ppermute(r1, axis_name='freq', perm=[(pp, pp ^ j0) for pp in range(af...]
    gather x0 -> x17, local copies, waits for them, and re-layouts: none -> 85.3 us
    all_to_all x1 -> x0, local copies, waits for them, and re-layouts: 62.7 us -> none  [local(): lax.all_to_all(crosses, 'freq', split_axis=2, concat_axis=1, tiled=True)]
    reshape x1 -> x0, local copies, waits for them, and re-layouts: 60.3 us -> none  [local(): grouped.reshape(count_slots, freq_total, stations_part, 2, double_width /...]
    another operation x0 -> x1, local copies, waits for them, and re-layouts: none -> 60.2 us  [local(): grouped.reshape(count_slots, freq_total, stations_part, 2, double_width /...]
    transpose x0 -> x1, local copies, waits for them, and re-layouts: none -> 52.5 us  [recast_the_chunk(): m = jnp.moveaxis(m, 0, row_dim)]
    unnamed x12 -> x18, local copies, waits for them, and re-layouts: 13.3 us -> 61.9 us
  transfers between devices with their start and end apart: 5 -> 7, of which waited for: 5 -> 6; matrix products, arithmetic and copies ran while one was open for 1% -> 1% of each run, Pallas kernels for 0% -> 0%
where the time goes in v1:
time: 1480 us
  waiting for transfers between devices  1010 us (68%)
  local copies, waits for them, and re-layouts  333 us (22%)
  other arithmetic  64.2 us (4%)
  matrix products  54.7 us (4%)
    ppermute x3, waiting for transfers between devices, local(): lax.ppermute(r1, axis_name='freq', perm=[(pp, pp ^ j0) for pp in range(af...  876 us
    ppermute x4, waiting for transfers between devices, from_behind(): lax.ppermute(shard, axis, [(i, (i + by) % size) for i in range(size)])  133 us
    unnamed x18, local copies, waits for them, and re-layouts  61.9 us
    another operation x1, local copies, waits for them, and re-layouts, local(): grouped.reshape(count_slots, freq_total, stations_part, 2, double_width /...  60.2 us
    gather x16, local copies, waits for them, and re-layouts  56.3 us
    transpose x1, local copies, waits for them, and re-layouts, recast_the_chunk(): m = jnp.moveaxis(m, 0, row_dim)  52.5 us
    dot_general x5, matrix products, cross_spectrum(): jnp.einsum('fks,fkt->fst', row_matrix, column_matrix, preferred_element_t...  32.5 us
  transfers between devices with their start and end apart: 7, of which 6 were waited for; matrix products, arithmetic and copies ran while one was open for 1% of the time, Pallas kernels for 0%

profile of v1, /device:TPU:6, one launch (start us, length us, event | category | flops | bytes accessed | tf_op | source)
XLA Modules:
  0.0 1478.8 jit_solution(6036326186744405290)
XLA Ops:
  18.1 28.2 %collective-permute-done = bf16[128,2,32,128]{3,2,1,0:T(8,128)(2,1)} collective-permute-done((bf16[128,2,32,128]{3,2,1,0:T(8,128)(2,1)}, bf16[128,2,32,128]{3,2,1,0:T(8,128)(2,1)}, u32[]{:S(2)}, u32[]{:S(2)}) %collective-permute-start) | collective-permute-done | bytes 2097184 | tf_op jit(solution)/shard_map/ppermute | solution.py:29
  49.6 44.5 %collective-permute-done.1 = bf16[128,2,32,128]{3,2,1,0:T(8,128)(2,1)} collective-permute-done((bf16[128,2,32,128]{3,2,1,0:T(8,128)(2,1)}, bf16[128,2,32,128]{3,2,1,0:T(8,128)(2,1)}, u32[]{:S(2)}, u32[]{:S(2)}) %collective-permute-start.1) | collective-permute-done | bytes 2097184 | tf_op jit(solution)/shard_map/ppermute | solution.py:29
  97.4 39.5 %collective-permute-done.2 = bf16[128,2,32,128]{3,2,1,0:T(8,128)(2,1)} collective-permute-done((bf16[128,2,32,128]{3,2,1,0:T(8,128)(2,1)}, bf16[128,2,32,128]{3,2,1,0:T(8,128)(2,1)}, u32[]{:S(2)}, u32[]{:S(2)}) %collective-permute-start.2) | collective-permute-done | bytes 2097184 | tf_op jit(solution)/shard_map/ppermute | solution.py:29
  140.3 21.1 %collective-permute-done.3 = bf16[128,2,32,128]{3,2,1,0:T(8,128)(2,1)S(1)} collective-permute-done((bf16[128,2,32,128]{3,2,1,0:T(8,128)(2,1)}, bf16[128,2,32,128]{3,2,1,0:T(8,128)(2,1)S(1)}, u32[]{:S(2)}, u32[]{:S(2)}) %collective-permute-start.3) | collective-permute-done | bytes 2097184 | tf_op jit(solution)/shard_map/ppermute | solution.py:29
  163.2 8.0 constant_dynamic-slice_fusion.2
  193.2 8.5 constant_dynamic-update-slice_fusion.5
  208.2 8.5 constant_dynamic-update-slice_fusion.4
  223.0 8.5 constant_dynamic-update-slice_fusion.3
  238.0 8.5 constant_dynamic-update-slice_fusion.2
  252.9 8.5 constant_dynamic-update-slice_fusion.1
  261.4 28.4 %dynamic-slice_bitcast_fusion.3 = (bf16[1,5,128,32,256]{4,3,2,1,0:T(8,128)(2,1)}, bf16[5,128,32,256]{3,2,1,0:T(8,128)(2,1)}, bf16[5,128,32,256]{3,2,1,0:T(8,128)(2,1)}, bf16[5,128,32,256]{3,2,1,0:T(8,128)(2,1)}) fusion(bf16[5,128,4,32,256]{4,3,2,1,0:T(8,128)(2,1)} %constant_dynamic-update-slice_fusion.1, s32[]{:T(128)S(6)} %select_n.110, s32[]{:T(128)S(6)} %select_n.113, ...), kind=kLoop, calls=%fused_computation.17 | loop fusion | bytes 83886096 | tf_op jit(solution)/shard_map/dynamic_slice | solution.py:73
  297.4 223.0 %collective-permute-done.6 = bf16[5,128,32,256]{3,2,1,0:T(8,128)(2,1)} collective-permute-done((bf16[5,128,32,256]{3,2,1,0:T(8,128)(2,1)}, bf16[5,128,32,256]{3,2,1,0:T(8,128)(2,1)}, u32[]{:S(2)}, u32[]{:S(2)}) %collective-permute-start.6) | collective-permute-done | bytes 10485792 | tf_op jit(solution)/shard_map/ppermute | solution.py:76
  520.3 653.0 %collective-permute-done.5 = bf16[5,128,32,256]{3,2,1,0:T(8,128)(2,1)} collective-permute-done((bf16[5,128,32,256]{3,2,1,0:T(8,128)(2,1)}, bf16[5,128,32,256]{3,2,1,0:T(8,128)(2,1)}, u32[]{:S(2)}, u32[]{:S(2)}) %collective-permute-start.5) | collective-permute-done | bytes 10485792 | tf_op jit(solution)/shard_map/ppermute | solution.py:76
  1173.4 28.1 %pad_maximum_fusion = bf16[4,5,128,32,256]{4,3,2,1,0:T(8,128)(2,1)} fusion(bf16[1,5,128,32,256]{4,3,2,1,0:T(8,128)(2,1)} %bitcast.47, bf16[1,5,128,32,256]{4,3,2,1,0:T(8,128)(2,1)} %bitcast.45, bf16[1,5,128,32,256]{4,3,2,1,0:T(8,128)(2,1)} %bitcast.43, bf16[1,5,128,32,256]{4,3,2,1,0:T(8,128)(2,1)} %get-tuple-element.39), kind=kLoop, calls=%fused_computation.4 | loop fusion | flops 62914560 | bytes 83886080 | tf_op jit(solution)/shard_map/stack | solution.py:78
  1201.5 29.1 %fusion.53 = (bf16[4,5,128,32,128]{4,3,2,1,0:T(8,128)(2,1)}, bf16[4,5,128,32,128]{4,3,2,1,0:T(8,128)(2,1)}) fusion(bf16[4,5,128,32,256]{4,3,2,1,0:T(8,128)(2,1)} %pad_maximum_fusion), kind=kLoop, calls=%fused_computation.110 | loop fusion | bytes 83886080 | tf_op jit(solution)/shard_map/gather | solution.py:79
  1230.5 7.3 broadcast.213.clone
  1237.8 28.2 %while.3 = (s32[]{:T(128)}, bf16[4,5,128,32,128]{4,3,2,1,0:T(8,128)(2,1)}, s32[4,1]{0,1:T(1,128)S(1)}, bf16[4,5,128,32,128]{4,3,2,1,0:T(8,128)(2,1)}, s32[]{:T(128)}) while((s32[]{:T(128)}, bf16[4,5,128,32,128]{4,3,2,1,0:T(8,128)(2,1)}, s32[4,1]{0,1:T(1,128)S(1)}, bf16[4,5,128,32,128]{4,3,2,1,0:T(8,128)(2,1)}, s32[]{:T(128)}) %tuple.47), condition=%wide.while_cond.1, body=%wide.while_body.1.sunk | while | flops 2 | bytes 10486357 | solution.py:79
  1266.0 7.3 broadcast.213.clone.1
  1273.3 28.1 %while.2 = (s32[]{:T(128)}, bf16[4,5,128,32,128]{4,3,2,1,0:T(8,128)(2,1)}, s32[4,1]{0,1:T(1,128)S(1)}, bf16[4,5,128,32,128]{4,3,2,1,0:T(8,128)(2,1)}, s32[]{:T(128)}) while((s32[]{:T(128)}, bf16[4,5,128,32,128]{4,3,2,1,0:T(8,128)(2,1)}, s32[4,1]{0,1:T(1,128)S(1)}, bf16[4,5,128,32,128]{4,3,2,1,0:T(8,128)(2,1)}, s32[]{:T(128)}) %tuple.53), condition=%wide.while_cond, body=%wide.while_body.sunk | while | flops 2 | bytes 10486357 | solution.py:79
  1301.4 28.3 %maximum_bitcast_fusion = bf16[5,4,128,32,256]{4,3,2,0,1:T(8,128)(2,1)} fusion(bf16[4,5,128,32,128]{4,3,2,1,0:T(8,128)(2,1)} %get-tuple-element.20, bf16[4,5,128,32,128]{4,3,2,1,0:T(8,128)(2,1)} %get-tuple-element.12), kind=kLoop, calls=%fused_computation.5 | loop fusion | flops 83886080 | bytes 83886080 | tf_op jit(solution)/shard_map/transpose | solution.py:22
  1329.7 52.5 %copy.9 = bf16[5,4,128,32,256]{2,1,4,3,0:T(4,128)(2,1)} copy(bf16[5,4,128,32,256]{4,3,2,0,1:T(8,128)(2,1)} %maximum_bitcast_fusion) | data formatting | bytes 83886080 | tf_op jit(solution)/shard_map/transpose | solution.py:22
  1382.2 60.2 %reshape_reshape.3 = bf16[5,512,32,2,128]{1,4,3,2,0:T(8,128)(2,1)} reshape(bf16[5,4,128,32,256]{2,1,4,3,0:T(4,128)(2,1)} %copy.9) | data formatting | bytes 83886080 | tf_op jit(solution)/shard_map/reshape;reshape | solution.py:82
  1442.5 22.1 %fusion.1 = bf16[1,5,32,256,128]{3,4,2,1,0:T(8,128)(2,1)} fusion(bf16[5,512,32,2,128]{1,4,3,2,0:T(8,128)(2,1)} %reshape_reshape.3, bf16[256,512,1]{1,0,2:T(8,128)(2,1)S(1)} %copy-done.3, bf16[256,512,1]{1,0,2:T(8,128)(2,1)S(1)} %copy-done.2), kind=kOutput, calls=%fused_computation.13 | convolution fusion | flops 10748166144 | bytes 52953088 | tf_op jit(solution)/shard_map/lfr,nfsrt->nslt/dot_general | solution.py:83
  1464.6 14.2 copy.10
  (60 shorter events, 131.1 us)
Async XLA Ops:
  0.0 46.3 %collective-permute-start = (bf16[128,2,32,128]{3,2,1,0:T(8,128)(2,1)}, bf16[128,2,32,128]{3,2,1,0:T(8,128)(2,1)}, u32[]{:S(2)}, u32[]{:S(2)}) collective-permute-start(bf16[128,2,32,128]{3,2,1,0:T(8,128)(2,1)} %bitcast.126), channel_id=1, source_target_pairs={{0,7},{1,0},{2,1},{3,2},{4,3},{5,4},{6,5},{7,6},{8,15},{9,8},{10,9... | collective-permute-start | bytes 6291464 | tf_op jit(solution)/shard_map/ppermute | solution.py:29
  0.0 94.1 %collective-permute-start.1 = (bf16[128,2,32,128]{3,2,1,0:T(8,128)(2,1)}, bf16[128,2,32,128]{3,2,1,0:T(8,128)(2,1)}, u32[]{:S(2)}, u32[]{:S(2)}) collective-permute-start(bf16[128,2,32,128]{3,2,1,0:T(8,128)(2,1)} %bitcast.127), channel_id=1, source_target_pairs={{0,6},{1,7},{2,0},{3,1},{4,2},{5,3},{6,4},{7,5},{8,14},{9,15},{10,... | collective-permute-start | bytes 6291464 | tf_op jit(solution)/shard_map/ppermute | solution.py:29
  1.4 135.6 %collective-permute-start.2 = (bf16[128,2,32,128]{3,2,1,0:T(8,128)(2,1)}, bf16[128,2,32,128]{3,2,1,0:T(8,128)(2,1)}, u32[]{:S(2)}, u32[]{:S(2)}) collective-permute-start(bf16[128,2,32,128]{3,2,1,0:T(8,128)(2,1)} %bitcast.128), channel_id=1, source_target_pairs={{0,5},{1,6},{2,7},{3,0},{4,1},{5,2},{6,3},{7,4},{8,13},{9,14},{10,... | collective-permute-start | bytes 6291464 | tf_op jit(solution)/shard_map/ppermute | solution.py:29
  1.4 160.0 %collective-permute-start.3 = (bf16[128,2,32,128]{3,2,1,0:T(8,128)(2,1)}, bf16[128,2,32,128]{3,2,1,0:T(8,128)(2,1)S(1)}, u32[]{:S(2)}, u32[]{:S(2)}) collective-permute-start(bf16[128,2,32,128]{3,2,1,0:T(8,128)(2,1)} %bitcast.129), channel_id=1, source_target_pairs={{0,4},{1,5},{2,6},{3,7},{4,0},{5,1},{6,2},{7,3},{8,12},{9,13},{10,... | collective-permute-start | bytes 6291464 | tf_op jit(solution)/shard_map/ppermute | solution.py:29
  171.1 3.2 copy-start
  181.7 4.7 copy-start.1
  289.8 230.5 %collective-permute-start.6 = (bf16[5,128,32,256]{3,2,1,0:T(8,128)(2,1)}, bf16[5,128,32,256]{3,2,1,0:T(8,128)(2,1)}, u32[]{:S(2)}, u32[]{:S(2)}) collective-permute-start(bf16[5,128,32,256]{3,2,1,0:T(8,128)(2,1)} %get-tuple-element.40), channel_id=1, source_target_pairs={{0,24},{8,16},{16,8},{24,0},{1,25},{9,17},{17,9},{25,1},{2,26},{10... | collective-permute-start | bytes 31457288 | tf_op jit(solution)/shard_map/ppermute | solution.py:76
  293.4 879.9 %collective-permute-start.5 = (bf16[5,128,32,256]{3,2,1,0:T(8,128)(2,1)}, bf16[5,128,32,256]{3,2,1,0:T(8,128)(2,1)}, u32[]{:S(2)}, u32[]{:S(2)}) collective-permute-start(bf16[5,128,32,256]{3,2,1,0:T(8,128)(2,1)} %get-tuple-element.41), channel_id=1, source_target_pairs={{0,16},{8,24},{16,0},{24,8},{1,17},{9,25},{17,1},{25,9},{2,18},{10... | collective-permute-start | bytes 31457288 | tf_op jit(solution)/shard_map/ppermute | solution.py:76
  293.4 879.9 %collective-permute-start.4 = (bf16[5,128,32,256]{3,2,1,0:T(8,128)(2,1)}, bf16[5,128,32,256]{3,2,1,0:T(8,128)(2,1)}, u32[]{:S(2)}, u32[]{:S(2)}) collective-permute-start(bf16[5,128,32,256]{3,2,1,0:T(8,128)(2,1)} %get-tuple-element.42), channel_id=1, source_target_pairs={{0,8},{8,0},{16,24},{24,16},{1,9},{9,1},{17,25},{25,17},{2,10},{10... | collective-permute-start | bytes 31457288 | tf_op jit(solution)/shard_map/ppermute | solution.py:76
  1382.2 60.3 %copy-start.2 = (bf16[256,512,1]{1,0,2:T(8,128)(2,1)S(1)}, bf16[256,512,1]{1,0,2:T(8,128)(2,1)}, u32[]{:S(2)}) copy-start(bf16[256,512,1]{1,0,2:T(8,128)(2,1)} %get-tuple-element.58) | copy-start | bytes 786436
  1382.2 60.3 %copy-start.3 = (bf16[256,512,1]{1,0,2:T(8,128)(2,1)S(1)}, bf16[256,512,1]{1,0,2:T(8,128)(2,1)}, u32[]{:S(2)}) copy-start(bf16[256,512,1]{1,0,2:T(8,128)(2,1)} %get-tuple-element.59) | copy-start | bytes 786436
